TPU v7x, 32 devices: a whole 2x2x4 slice. The times are simulated.
32 devices in a mesh: req: 8 (over z, y), tp: 4 (over x, core).
Axes of the slice: x: 2, y: 2, z: 4, core: 2. Of those that a mesh axis runs over, the one named last changes fastest.
Arguments:
- hidden: bfloat16 [32, 128, 2304], P('req', None, 'tp')
- qkv: bfloat16 [32, 128, 4, 1024], P('req', None, 'tp')
- page_store: bfloat16 [16, 128, 4, 512], P('req', None, 'tp')
- page_owner: int32 [8], replicated, may hold values from 0 to 7, as said below
- page_slot: int32 [8], replicated, may hold values from 0 to 1
- lengths: int32 [32], replicated, may hold values from 1 to 128, 2048 in all
- request_perm: int32 [32], replicated, may hold values from 0 to 31, each once
- w_out: bfloat16 [2048, 2304], P(None, 'tp')
- post_gain: float32 [2304], P('tp'), may hold values from 0.25 to 1.75
Outputs:
- result: bfloat16 [32, 128, 2304], P('req', None, 'tp')
Inputs may be any that keep to these rules, and one draw needn't show every extreme that they name: Page p lies in slot page_slot[p] of the device with index page_owner[p] along req; no two pages share an owner.
All inputs are finite; a program needn't handle non-finite values.
Results may differ from a plain program's by a relative error of at most 0.0043.
Values may be sent and summed in bfloat16 or wider, within the bound.
No kernel may reach another device: no remote copies, remote signals or barrier semaphores. Data moves between devices by JAX's collectives and lax.ppermute only.
A program may use at most 64 MiB of HBM per device.

v0:
```python
import jax
import jax.numpy as jnp
from jax import lax
from jax.sharding import PartitionSpec as P

D = 2304
HD = 256
EPSILON = 1e-06
SOFT_CAP = 50.0


def tables(positions, width):
    half_width = width // 2
    frequency = 10000.0 ** (-(jnp.arange(half_width, dtype=jnp.float32) * 2.0 / width))
    angles = positions.astype(jnp.float32)[:, None] * frequency[None, :]
    return (jnp.cos(angles), jnp.sin(angles))


def rotate(values, cosine, sine):
    half_width = values.shape[-1] // 2
    first = values[..., :half_width]
    second = values[..., half_width:]
    return jnp.concatenate([first * cosine - second * sine, second * cosine + first * sine], -1)


def capped_exp(scores):
    return jnp.exp(SOFT_CAP * jnp.tanh(scores / SOFT_CAP))


def on_device(
    hidden, qkv, page_store, page_owner, page_slot, lengths, request_perm, w_out, post_gain
):
    requests, slots, local_width = hidden.shape
    groups = qkv.shape[2]
    per_group = qkv.shape[3] // HD - 2
    token_rows = requests * slots
    device_row = lax.axis_index("req")
    my_requests = lax.dynamic_slice_in_dim(request_perm, device_row * requests, requests)
    matches = my_requests[:, None] == jnp.arange(lengths.shape[0], dtype=jnp.int32)[None, :]
    my_lengths = jnp.sum(jnp.where(matches, lengths[None, :], 0), 1)
    position = jnp.arange(slots, dtype=jnp.int32)
    live_mask = (position[None, :] < my_lengths[:, None]).astype(jnp.float32)
    source = hidden.astype(jnp.float32)
    projections = qkv.astype(jnp.float32).reshape(requests, slots, groups, per_group + 2, HD)
    page_count = page_owner.shape[0]
    prefix_len = page_store.shape[1] * page_count
    cosine, sine = tables(prefix_len + position, HD)
    queries = (
        rotate(
            projections[:, :, :, :per_group],
            cosine[None, :, None, None, :],
            sine[None, :, None, None, :],
        )
        * HD ** (-0.5)
    ).astype(jnp.bfloat16)
    fresh_keys = rotate(
        projections[:, :, :, per_group], cosine[None, :, None, :], sine[None, :, None, :]
    ).astype(jnp.bfloat16)
    fresh_values = projections[:, :, :, per_group + 1].astype(jnp.bfloat16)
    picked = page_store[page_slot]
    held_here = page_owner == device_row
    offered = jnp.where(held_here[:, None, None, None], picked.astype(jnp.float32), 0.0)
    prefix = lax.psum(offered, "req").astype(jnp.bfloat16)
    prefix = prefix.reshape(prefix_len, groups, 2 * HD)
    prefix_keys = prefix[:, :, :HD]
    prefix_values = prefix[:, :, HD:]
    prefix_weights = capped_exp(
        jnp.einsum("rsgqh,tgh->rsgqt", queries, prefix_keys, preferred_element_type=jnp.float32)
    )
    allowed = (position[None, None, :] <= position[None, :, None]) & (
        position[None, None, :] < my_lengths[:, None, None]
    )
    suffix_raw = capped_exp(
        jnp.einsum("rsgqh,rtgh->rsgqt", queries, fresh_keys, preferred_element_type=jnp.float32)
    )
    suffix_weights = jnp.where(allowed[:, :, None, None, :], suffix_raw, 0.0)
    totals = jnp.sum(prefix_weights, -1) + jnp.sum(suffix_weights, -1)
    prefix_probs = (prefix_weights / totals[..., None]).astype(jnp.bfloat16)
    suffix_probs = (suffix_weights / totals[..., None]).astype(jnp.bfloat16)
    attended = jnp.einsum(
        "rsgqt,tgh->rsgqh", prefix_probs, prefix_values, preferred_element_type=jnp.float32
    )
    attended = attended + jnp.einsum(
        "rsgqt,rtgh->rsgqh", suffix_probs, fresh_values, preferred_element_type=jnp.float32
    )
    attended = attended.astype(jnp.bfloat16).reshape(token_rows, groups * per_group * HD)
    projected = jnp.dot(
        lax.all_gather(attended, "tp", axis=1, tiled=True),
        w_out,
        preferred_element_type=jnp.float32,
    )
    projected = projected.reshape(requests, slots, local_width)
    branch_total = lax.psum(jnp.sum(projected * projected, -1), "tp")
    branch = projected * lax.rsqrt(branch_total / D + EPSILON)[..., None] * post_gain
    return ((source + branch) * live_mask[..., None]).astype(jnp.bfloat16)


def solution(mesh):
    placed = (
        P("req", None, "tp"),
        P("req", None, "tp", None),
        P("req", None, "tp", None),
        P(),
        P(),
        P(),
        P(),
        P(None, "tp"),
        P("tp"),
    )
    return jax.shard_map(
        on_device, mesh=mesh, in_specs=placed, out_specs=P("req", None, "tp"), check_vma=False
    )
```

profile of v0, /device:TPU:0, one launch (start us, length us, event | category | flops | bytes accessed | tf_op | source)
XLA Modules:
  0.0 157.9 jit_solution(3614587715875364756)
XLA Ops:
  6.5 0.0 copy-start
  6.5 0.0 all-gather.2.cloned.1.call-start
  6.6 0.8 broadcast_compare_fusion
  7.4 0.7 compare_select_fusion
  8.1 0.7 dynamic_slice.3
  8.8 0.8 select_reduce_fusion
  9.6 0.1 fusion.36
  9.7 1.6 gather_fusion
  11.3 1.7 %convert_select_fusion = f32[8,128,1,512]{3,1,0,2:T(8,128)} fusion(bf16[8,128,512]{2,1,0:T(8,128)(2,1)S(1)} %gather_fusion, pred[8]{0:T(512)(128)(4,1)S(1)} %broadcast_compare_fusion), kind=kLoop, calls=%fused_computation.5 | loop fusion | flops 1048576 | bytes 3145736 | tf_op jit(solution)/shard_map/jit(_where)/select_n | solution.py:62
  13.0 0.0 copy-start.2
  13.0 95.0 %all-reduce.1 = bf16[8,128,1,512]{3,1,0,2:T(8,128)(2,1)} all-reduce(f32[8,128,1,512]{3,1,0,2:T(8,128)} %convert_select_fusion), channel_id=1, replica_groups=mesh['req'=8,'tp'=4] {'req'}, use_global_device_ids=true, to_apply=%region_0.1 | all-reduce | flops 524288 | bytes 3145728 | tf_op jit(solution)/shard_map/psum | solution.py:63
  108.0 0.0 copy-done.2
  108.0 1.3 copy.24
  109.3 1.5 copy.25
  110.8 0.2 reshape.303
  111.0 0.0 copy-start.1
  111.0 0.3 multiply_cosine_fusion
  111.4 0.1 subtract_bitcast_fusion
  111.5 0.1 fusion.25
  111.6 0.1 broadcast_and_fusion
  111.7 0.5 copy-done.1
  112.2 1.3 bitcast_reduce_fusion
  113.6 0.4 fusion.37
  114.0 1.5 fusion.6
  115.5 1.2 fusion.10
  116.7 0.5 copy.31
  117.2 0.9 copy.43
  118.1 0.0 all-gather.2.cloned.1.call-update
  118.1 0.0 copy-start.3
  118.1 21.8 %all-gather.2.cloned.1.call-done = bf16[512,2048]{1,0:T(8,128)(2,1)} async-done(((bf16[512,512]{1,0:T(8,128)(2,1)}), bf16[512,2048]{1,0:T(8,128)(2,1)}) %all-gather.2.cloned.1.call-update) | async-done | bytes 2097168 | tf_op jit(solution)/shard_map/all_gather | solution.py:88
  139.9 0.0 copy-done
  139.9 3.0 %multiply_reduce_fusion = (f32[512]{0:T(512)S(1)}, f32[512,576]{0,1:T(8,128)S(1)}) fusion(bf16[512,2048]{1,0:T(8,128)(2,1)} %all-gather.2.cloned.1.call-done, bf16[2048,576]{0,1:T(8,128)(2,1)S(1)} %copy-done), kind=kOutput, calls=%fused_computation.24 | convolution fusion | flops 1208548864 | bytes 5638144 | tf_op jit(solution)/shard_map/dot_general | solution.py:87
  143.0 5.9 %psum.15 = f32[4,128]{1,0:T(4,128)S(1)} all-reduce(f32[4,128]{1,0:T(4,128)S(1)} %bitcast.112), channel_id=1, replica_groups=mesh['req'=8,'tp'=4] {'tp'}, use_global_device_ids=true, to_apply=%region_5.6 | all-reduce | flops 512 | bytes 4096 | tf_op jit(solution)/shard_map/psum | solution.py:93
  148.9 0.0 copy-done.3
  148.9 2.2 %fusion.18 = bf16[4,128,576]{1,2,0:T(8,128)(2,1)} fusion(bf16[4,128,576]{1,2,0:T(8,128)(2,1)} %param.9, f32[4,128]{1,0:T(4,128)S(1)} %get-tuple-element.11, f32[576]{0:T(1024)S(1)} %copy-done.3, f32[4,128]{1,0:T(4,128)S(1)} %add_rsqrt_fusion, f32[512,576]{0,1:T(8,128)S(1)} %get-tuple-element.18), kind=kLoop, calls=%fused_computation.23 | loop fusion | flops 1769472 | bytes 2365696 | tf_op jit(solution)/shard_map/convert_element_type | solution.py:95
  (7 shorter events, 0.1 us)
Async XLA Ops:
  6.5 133.4 %copy-start = (bf16[2048,576]{0,1:T(8,128)(2,1)S(1)}, bf16[2048,576]{0,1:T(8,128)(2,1)}, u32[]{:S(2)}) copy-start(bf16[2048,576]{0,1:T(8,128)(2,1)} %param.16) | copy-start | bytes 7077892
  6.5 133.4 %all-gather.2.cloned.1.call-start = ((), (), s32[]{:S(2)}) async-start(), calls=%async_computation | async-start | bytes 2621440 | tf_op jit(solution)/shard_map/all_gather | solution.py:88
  13.0 95.0 %copy-start.2 = (bf16[4,128,1,1024]{3,1,2,0:T(8,128)(2,1)S(1)}, bf16[4,128,1,1024]{3,1,2,0:T(8,128)(2,1)}, u32[]{:S(2)}) copy-start(bf16[4,128,1,1024]{3,1,2,0:T(8,128)(2,1)} %param.10) | copy-start | bytes 3145732
  111.0 1.2 copy-start.1
  118.1 30.8 %copy-start.3 = (f32[576]{0:T(1024)S(1)}, f32[576]{0:T(1024)}, u32[]{:S(2)}) copy-start(f32[576]{0:T(1024)} %param.17) | copy-start | bytes 6916
Sparse Core Ops, SparseCore 0:
  118.2 21.6 all-gather.1
where the time goes:
time: 158 us
  blocking collectives  101 us (64%)
  waiting for transfers between devices  21.9 us (14%)
  between operations  13.5 us (9%)
  matrix products  7.48 us (5%)
  other arithmetic  7.23 us (5%)
  local copies, waits for them, and re-layouts  6.97 us (4%)
    psum x1, blocking collectives, on_device(): prefix = lax.psum(offered, 'req').astype(jnp.bfloat16)  95 us
    all_gather x1, waiting for transfers between devices, on_device(): lax.all_gather(attended, 'tp', axis=1, tiled=True)  21.8 us
    psum x1, blocking collectives, on_device(): branch_total = lax.psum(jnp.sum(projected * projected, -1), 'tp')  5.89 us
  transfers between devices with their start and end apart: 1, of which 1 were waited for; matrix products, arithmetic and copies ran while one was open for 0% of the time, Pallas kernels for 0%

commit v1 on v0

--- a/solution.py
+++ b/solution.py
@@ -7,6 +7,19 @@
 HD = 256
 EPSILON = 1e-06
 SOFT_CAP = 50.0
+
+
+def gather_around(x, axis, dim):
+    ways = lax.axis_size(axis)
+    up = [(d, (d + 1) % ways) for d in range(ways)]
+    down = [(d, (d - 1) % ways) for d in range(ways)]
+    earlier, later = ([x], [x])
+    for _ in range(ways // 2):
+        earlier.append(lax.ppermute(earlier[-1], axis, up))
+    for _ in range((ways - 1) // 2):
+        later.append(lax.ppermute(later[-1], axis, down))
+    line = jnp.concatenate([*earlier[::-1], *later[1:]], axis=dim)
+    return jnp.roll(line, (lax.axis_index(axis) - ways // 2) * x.shape[dim], axis=dim)
 
 
 def tables(positions, width):
@@ -84,11 +97,7 @@
         "rsgqt,rtgh->rsgqh", suffix_probs, fresh_values, preferred_element_type=jnp.float32
     )
     attended = attended.astype(jnp.bfloat16).reshape(token_rows, groups * per_group * HD)
-    projected = jnp.dot(
-        lax.all_gather(attended, "tp", axis=1, tiled=True),
-        w_out,
-        preferred_element_type=jnp.float32,
-    )
+    projected = jnp.dot(gather_around(attended, "tp", 1), w_out, preferred_element_type=jnp.float32)
     projected = projected.reshape(requests, slots, local_width)
     branch_total = lax.psum(jnp.sum(projected * projected, -1), "tp")
     branch = projected * lax.rsqrt(branch_total / D + EPSILON)[..., None] * post_gain

time: 158 us -> 149 us (0.943)
  between operations: 13.5 us -> 0.23 us
  local copies, waits for them, and re-layouts: 6.97 us -> 11.5 us
  waiting for transfers between devices: 21.9 us -> 19.4 us
  starting transfers between devices: 0.01 us -> 1.8 us
    all_gather x1 -> x0, waiting for transfers between devices: 21.8 us -> none  [on_device(): lax.all_gather(attended, 'tp', axis=1, tiled=True)]
    ppermute x0 -> x3, waiting for transfers between devices: none -> 19.4 us  [the longest x2 19.4 us: gather_around(): earlier.append(lax.ppermute(earlier[-1], axis, up))]
    unnamed x10 -> x15, local copies, waits for them, and re-layouts: 2.71 us -> 6.16 us
    ppermute x0 -> x3, starting transfers between devices: none -> 1.8 us  [the longest x1 1.74 us: gather_around(): later.append(lax.ppermute(later[-1], axis, down))]
  transfers between devices with their start and end apart: 1 -> 3, of which waited for: 1 -> 2; matrix products, arithmetic and copies ran while one was open for 0% -> 1% of each run, Pallas kernels for 0% -> 0%
where the time goes in v1:
time: 149 us; the launch traced here: 148 us
  blocking collectives  102 us (68%)
  waiting for transfers between devices  19.4 us (13%)
  local copies, waits for them, and re-layouts  11.5 us (8%)
  other arithmetic  7.18 us (5%)
  matrix products  5.97 us (4%)
  starting transfers between devices  1.8 us (1%)
    psum x1, blocking collectives, on_device(): prefix = lax.psum(offered, 'req').astype(jnp.bfloat16)  94.8 us
    ppermute x2, waiting for transfers between devices, gather_around(): earlier.append(lax.ppermute(earlier[-1], axis, up))  19.4 us
    psum x1, blocking collectives, on_device(): branch_total = lax.psum(jnp.sum(projected * projected, -1), 'tp')  7.04 us
    unnamed x15, local copies, waits for them, and re-layouts  6.16 us
  transfers between devices with their start and end apart: 3, of which 2 were waited for; matrix products, arithmetic and copies ran while one was open for 1% of the time, Pallas kernels for 0%

profile of v1, /device:TPU:0, one launch (start us, length us, event | category | flops | bytes accessed | tf_op | source)
XLA Modules:
  0.0 148.0 jit_solution(11768755042611466080)
XLA Ops:
  0.0 0.0 copy-start
  0.0 0.8 broadcast_compare_fusion
  0.9 0.7 compare_select_fusion
  1.5 0.7 dynamic_slice.7
  2.2 0.8 select_reduce_fusion
  3.1 0.1 fusion.39
  3.2 1.6 %gather_fusion = bf16[8,128,512]{2,1,0:T(8,128)(2,1)S(1)} fusion(bf16[2,128,512]{2,1,0:T(8,128)(2,1)} %bitcast.108, s32[1024]{0:T(1024)S(1)} %pad_clamp_fusion), kind=kCustom, calls=%fused_computation | custom fusion | bytes 2097184 | tf_op jit(solution)/shard_map/gather | solution.py:73
  4.7 1.7 %convert_select_fusion = f32[8,128,1,512]{3,1,0,2:T(8,128)} fusion(bf16[8,128,512]{2,1,0:T(8,128)(2,1)S(1)} %gather_fusion, pred[8]{0:T(512)(128)(4,1)S(1)} %broadcast_compare_fusion), kind=kLoop, calls=%fused_computation.5 | loop fusion | flops 1048576 | bytes 3145736 | tf_op jit(solution)/shard_map/jit(_where)/select_n | solution.py:75
  6.5 94.8 %all-reduce.1 = bf16[8,128,1,512]{3,1,0,2:T(8,128)(2,1)} all-reduce(f32[8,128,1,512]{3,1,0,2:T(8,128)} %convert_select_fusion), channel_id=1, replica_groups=mesh['req'=8,'tp'=4] {'req'}, use_global_device_ids=true, to_apply=%region_0.1 | all-reduce | flops 524288 | bytes 3145728 | tf_op jit(solution)/shard_map/psum | solution.py:76
  101.3 2.3 %copy.24 = bf16[4,128,1,1024]{1,3,0,2:T(8,128)(2,1)} copy(bf16[4,128,1,1024]{3,1,2,0:T(8,128)(2,1)} %param.10) | data formatting | bytes 2097152 | tf_op args[1]
  103.6 1.5 %copy.25 = bf16[4,128,1,4,256]{4,1,3,0,2:T(8,128)(2,1)S(1)} copy(bf16[4,128,1,4,256]{1,4,3,0,2:T(8,128)(2,1)} %bitcast.109) | data formatting | bytes 2097152 | tf_op jit(solution)/shard_map/reshape | solution.py:57
  105.1 0.0 copy-start.1
  105.1 0.2 reshape.303
  105.3 0.3 multiply_cosine_fusion
  105.7 0.1 subtract_bitcast_fusion
  105.8 0.1 fusion.27
  105.9 0.1 broadcast_and_fusion
  106.0 0.3 copy-done.1
  106.3 1.3 bitcast_reduce_fusion
  107.6 0.4 fusion.40
  108.0 1.5 %fusion.8 = f32[4,128,1,2,256]{1,4,3,0,2:T(8,128)S(1)} fusion(f32[4,128,2]{1,2,0:T(2,128)S(1)} %add.78, f32[1024,4,128,2]{2,0,3,1:T(8,128)S(1)} %get-tuple-element.14, bf16[1024,1,512]{2,0,1:T(8,128)(2,1)S(1)} %bitcast.113), kind=kOutput, calls=%fused_computation.13 | convolution fusion | flops 541065216 | bytes 5771264 | tf_op jit(solution)/shard_map/rsgqt,tgh->rsgqh/dot_general | solution.py:93
  109.5 1.3 fusion.12
  110.8 0.5 copy.31
  111.2 0.1 copy.43
  111.3 0.1 collective-permute-start
  111.4 8.6 %collective-permute-done = bf16[512,512]{1,0:T(8,128)(2,1)S(1)} collective-permute-done((bf16[512,512]{1,0:T(8,128)(2,1)S(1)}, bf16[512,512]{1,0:T(8,128)(2,1)S(1)}, u32[]{:S(2)}, u32[]{:S(2)}) %collective-permute-start) | collective-permute-done | bytes 524320 | tf_op jit(solution)/shard_map/ppermute | solution.py:18
  120.0 0.0 collective-permute-start.1
  120.0 1.7 %collective-permute-start.2 = (bf16[512,512]{1,0:T(8,128)(2,1)S(1)}, bf16[512,512]{1,0:T(8,128)(2,1)}, u32[]{:S(2)}, u32[]{:S(2)}) collective-permute-start(bf16[512,512]{1,0:T(8,128)(2,1)S(1)} %bitcast.105), channel_id=1, source_target_pairs={{0,3},{1,0},{2,1},{3,2},{4,7},{5,4},{6,5},{7,6},{8,11},{9,8},{10,9... | collective-permute-start | bytes 1572872 | tf_op jit(solution)/shard_map/ppermute | solution.py:20
  121.7 10.8 %collective-permute-done.1 = bf16[512,512]{1,0:T(8,128)(2,1)} collective-permute-done((bf16[512,512]{1,0:T(8,128)(2,1)S(1)}, bf16[512,512]{1,0:T(8,128)(2,1)}, u32[]{:S(2)}, u32[]{:S(2)}) %collective-permute-start.1) | collective-permute-done | bytes 524320 | tf_op jit(solution)/shard_map/ppermute | solution.py:18
  132.5 1.1 constant_dynamic-update-slice_fusion.7
  133.6 0.1 constant_dynamic-update-slice_fusion.6
  133.7 0.1 constant_dynamic-update-slice_fusion.5
  133.8 0.0 collective-permute-done.2
  133.8 1.1 constant_dynamic-update-slice_fusion.4
  134.9 1.1 constant_dynamic-update-slice_fusion.3
  136.0 0.1 constant_dynamic-update-slice_fusion.2
  136.0 0.1 constant_dynamic-update-slice_fusion.1
  136.1 1.1 constant_dynamic-update-slice_fusion
  137.2 0.0 copy-done
  137.2 0.0 copy-start.2
  137.2 1.5 %multiply_reduce_fusion = (f32[512]{0:T(512)S(1)}, f32[512,576]{0,1:T(8,128)S(1)}) fusion(bf16[2048,576]{0,1:T(8,128)(2,1)S(1)} %copy-done, bf16[512,4096]{1,0:T(8,128)(2,1)S(1)} %constant_dynamic-update-slice_fusion, s32[]{:T(128)S(6)} %select_n.45), kind=kOutput, calls=%fused_computation.26 | convolution fusion | flops 1208548864 | bytes 5638148 | tf_op jit(solution)/shard_map/dot_general | solution.py:100
  138.8 7.0 %psum.15 = f32[4,128]{1,0:T(4,128)S(1)} all-reduce(f32[4,128]{1,0:T(4,128)S(1)} %bitcast.114), channel_id=1, replica_groups=mesh['req'=8,'tp'=4] {'tp'}, use_global_device_ids=true, to_apply=%region_5.6 | all-reduce | flops 512 | bytes 4096 | tf_op jit(solution)/shard_map/psum | solution.py:102
  145.8 0.0 copy-done.2
  145.8 2.2 %fusion.20 = bf16[4,128,576]{1,2,0:T(8,128)(2,1)} fusion(bf16[4,128,576]{1,2,0:T(8,128)(2,1)} %param.9, f32[4,128]{1,0:T(4,128)S(1)} %get-tuple-element.11, f32[576]{0:T(1024)S(1)} %copy-done.2, f32[4,128]{1,0:T(4,128)S(1)} %add_rsqrt_fusion, f32[512,576]{0,1:T(8,128)S(1)} %get-tuple-element.18), kind=kLoop, calls=%fused_computation.25 | loop fusion | flops 1769472 | bytes 2365696 | tf_op jit(solution)/shard_map/convert_element_type | solution.py:104
  (7 shorter events, 0.1 us)
Async XLA Ops:
  0.0 137.2 %copy-start = (bf16[2048,576]{0,1:T(8,128)(2,1)S(1)}, bf16[2048,576]{0,1:T(8,128)(2,1)}, u32[]{:S(2)}) copy-start(bf16[2048,576]{0,1:T(8,128)(2,1)} %param.16) | copy-start | bytes 7077892
  105.1 1.2 copy-start.1
  111.3 8.7 %collective-permute-start = (bf16[512,512]{1,0:T(8,128)(2,1)S(1)}, bf16[512,512]{1,0:T(8,128)(2,1)S(1)}, u32[]{:S(2)}, u32[]{:S(2)}) collective-permute-start(bf16[512,512]{1,0:T(8,128)(2,1)S(1)} %bitcast.104), channel_id=1, source_target_pairs={{0,1},{1,2},{2,3},{3,0},{4,5},{5,6},{6,7},{7,4},{8,9},{9,10},{10,1... | collective-permute-start | bytes 1572872 | tf_op jit(solution)/shard_map/ppermute | solution.py:18
  120.0 12.5 %collective-permute-start.1 = (bf16[512,512]{1,0:T(8,128)(2,1)S(1)}, bf16[512,512]{1,0:T(8,128)(2,1)}, u32[]{:S(2)}, u32[]{:S(2)}) collective-permute-start(bf16[512,512]{1,0:T(8,128)(2,1)S(1)} %collective-permute-done), channel_id=1, source_target_pairs={{0,1},{1,2},{2,3},{3,0},{4,5},{5,6},{6,7},{7,4},{8,9},{9,10},{10,1... | collective-permute-start | bytes 1572872 | tf_op jit(solution)/shard_map/ppermute | solution.py:18
  120.0 13.8 %collective-permute-start.2 = (bf16[512,512]{1,0:T(8,128)(2,1)S(1)}, bf16[512,512]{1,0:T(8,128)(2,1)}, u32[]{:S(2)}, u32[]{:S(2)}) collective-permute-start(bf16[512,512]{1,0:T(8,128)(2,1)S(1)} %bitcast.105), channel_id=1, source_target_pairs={{0,3},{1,0},{2,1},{3,2},{4,7},{5,4},{6,5},{7,6},{8,11},{9,8},{10,9... | collective-permute-start | bytes 1572872 | tf_op jit(solution)/shard_map/ppermute | solution.py:20
  137.2 8.6 %copy-start.2 = (f32[576]{0:T(1024)S(1)}, f32[576]{0:T(1024)}, u32[]{:S(2)}) copy-start(f32[576]{0:T(1024)} %param.17) | copy-start | bytes 6916
